TPU v7x, 512 devices: a whole 4x4x16 slice. The times are simulated.
512 devices in a mesh: row: 32 (over z_lo, x), col: 16 (over y, z_hi, core).
Axes of the slice: x: 4, y: 4, z: 16 (z_hi: 2, z_lo: 8; z = z_hi * 8 + z_lo), core: 2. Of those that a mesh axis runs over, the one named last changes fastest.
Arguments:
- anc_inv: bfloat16 [16384, 16384], P('row', 'col'), may hold values from -0.0546875 to 0.0546875
- panel: bfloat16 [1, 12288, 2048], P(None, 'col', 'row'), may hold values from -6 to 6
- structure: int32 [1, 96], replicated, may hold values from 0 to 127, as said below
Outputs:
- off_inv: float32 [1, 16384, 2048], P(None, 'row', 'col')
Inputs may be any that keep to these rules, and one draw needn't show every extreme that they name: Each structure[s] holds 96 distinct ancestor block indices, in the order in which the panel stores its row blocks (not sorted); each group of 8 consecutive ancestor blocks holds 5 to 7 of them, and some group of each supernode holds exactly 7.
All inputs are finite; a program needn't handle non-finite values.
Results may differ from a plain program's by a relative error of at most 0.0003.
Values may be sent and summed in bfloat16 or wider, within the bound.
No kernel may reach another device: no remote copies, remote signals or barrier semaphores. Data moves between devices by JAX's collectives and lax.ppermute only.
A program may use at most 64 MiB of HBM per device.

v0:
```python
import jax
import jax.numpy as jnp
from jax import lax
from jax.sharding import PartitionSpec as P

BS = 128
SBLK = 96


def body(anc_inv, panel, structure):
    col_index = lax.axis_index("col")
    row_index = lax.axis_index("row")
    local_rows, local_cols = anc_inv.shape
    group_blocks = local_cols // BS
    local_width = panel.shape[2]
    gathered = lax.all_gather(panel, "col", axis=1, tiled=True)
    own_blocks = row_index * (local_rows // BS) + jnp.arange(local_rows // BS, dtype=jnp.int32)
    block_ids = jnp.arange(group_blocks, dtype=jnp.int32)
    blocks_of = structure[0]
    compact = gathered[0].reshape(SBLK, BS * local_width)
    local_block = blocks_of - col_index * group_blocks
    picker = (local_block[None, :] == block_ids[:, None]).astype(jnp.bfloat16)
    picked = (
        jnp.dot(picker, compact, preferred_element_type=jnp.float32)
        .astype(jnp.bfloat16)
        .reshape(group_blocks * BS, local_width)
    )
    partial_value = jnp.dot(
        anc_inv,
        lax.all_gather(picked, "row", axis=1, tiled=True),
        preferred_element_type=jnp.float32,
    )
    summed = lax.psum_scatter(partial_value, "col", scatter_dimension=1, tiled=True)
    member = jnp.any(blocks_of[None, :] == own_blocks[:, None], axis=1)
    row_mask = jnp.repeat(member, BS)
    results = [jnp.where(row_mask[:, None], -summed, jnp.zeros_like(summed))]
    return jnp.stack(results)


def solution(mesh):
    in_specs = (P("row", "col"), P(None, "col", "row"), P())
    out_specs = P(None, "row", "col")
    return jax.shard_map(body, mesh=mesh, in_specs=in_specs, out_specs=out_specs, check_vma=False)
```

profile of v0, /device:TPU:2, one launch (start us, length us, event | category | flops | bytes accessed | tf_op | source)
XLA Modules:
  0.0 496.0 jit_solution(13682171453870324515)
XLA Ops:
  6.5 0.0 copy-start
  6.5 0.0 all-gather.3.cloned.1.call-start
  6.5 0.7 all-gather.3.cloned.1.call-update
  7.3 0.0 all-gather.5.cloned.1.call-start
  7.3 0.7 subtract_bitcast_fusion
  8.0 92.1 %all-gather.3.cloned.1.call-done = bf16[1,12288,64]{1,2,0:T(8,128)(2,1)} async-done(((bf16[1,768,64]{1,2,0:T(8,128)(2,1)}), bf16[1,12288,64]{1,2,0:T(8,128)(2,1)}) %all-gather.3.cloned.1.call-update) | async-done | bytes 1572880 | tf_op jit(solution)/shard_map/all_gather | solution.py:16
  100.1 4.1 copy.10
  104.2 4.3 reshape_squeeze.3
  108.4 0.3 convolution_convert_fusion
  108.7 0.3 reshape.8
  109.0 0.8 copy.11
  109.8 0.0 all-gather.5.cloned.1.call-update
  109.8 0.0 reduce-scatter.2.cloned.1.call-start
  109.9 218.6 %all-gather.5.cloned.1.call-done = bf16[1024,2048]{0,1:T(8,128)(2,1)} async-done(((bf16[1024,64]{0,1:T(8,128)(2,1)}), bf16[1024,2048]{0,1:T(8,128)(2,1)}) %all-gather.5.cloned.1.call-update) | async-done | bytes 4194320 | tf_op jit(solution)/shard_map/all_gather | solution.py:30
  328.5 0.0 copy-done
  328.5 6.5 %convolution_bitcast_fusion = f32[512,2048]{0,1:T(8,128)} fusion(bf16[1024,2048]{0,1:T(8,128)(2,1)} %all-gather.5.cloned.1.call-done, bf16[512,1024]{1,0:T(8,128)(2,1)S(1)} %copy-done), kind=kOutput, calls=%fused_computation.1 | convolution fusion | flops 2147483648 | bytes 9437184 | tf_op jit(solution)/shard_map/dot_general | solution.py:28
  335.0 0.0 copy-start.1
  335.0 0.0 reduce-scatter.2.cloned.1.call-update
  335.0 0.6 copy-done.1
  335.6 0.2 compare_reduce_fusion
  335.8 0.1 broadcast_bitcast_fusion
  335.9 151.7 %reduce-scatter.2.cloned.1.call-done = f32[512,128]{0,1:T(8,128)} async-done(((f32[512,2048]{0,1:T(8,128)}), f32[512,128]{0,1:T(8,128)}) %reduce-scatter.2.cloned.1.call-update) | async-done | bytes 262160 | tf_op jit(solution)/shard_map/reduce_scatter | solution.py:33
  487.6 1.0 select_bitcast_fusion
  488.6 0.8 copy.12
  (1 shorter events, 0.0 us)
Async XLA Ops:
  6.5 321.9 %copy-start = (bf16[512,1024]{1,0:T(8,128)(2,1)S(1)}, bf16[512,1024]{1,0:T(8,128)(2,1)}, u32[]{:S(2)}) copy-start(bf16[512,1024]{1,0:T(8,128)(2,1)} %param.3) | copy-start | bytes 3145732
  6.5 93.5 %all-gather.3.cloned.1.call-start = ((), (), s32[]{:S(2)}) async-start(), calls=%async_computation.1 | async-start | bytes 1671168 | tf_op jit(solution)/shard_map/all_gather | solution.py:16
  7.3 321.2 %all-gather.5.cloned.1.call-start = ((), (), s32[]{:S(2)}) async-start(), calls=%async_computation.2 | async-start | bytes 4325376 | tf_op jit(solution)/shard_map/all_gather | solution.py:30
  109.8 377.8 %reduce-scatter.2.cloned.1.call-start = ((), (), s32[]{:S(2)}) async-start(), calls=%async_computation.3 | async-start | bytes 4456448 | tf_op jit(solution)/shard_map/reduce_scatter | solution.py:33
  335.0 0.7 copy-start.1
Sparse Core Ops, SparseCore 0:
  10.6 89.3 all-gather.2
  109.9 218.4 all-gather.4
  335.1 152.4 reduce-scatter.1
where the time goes:
time: 496 us
  waiting for transfers between devices  463 us (93%)
  between operations  13.2 us (3%)
  local copies, waits for them, and re-layouts  11 us (2%)
  matrix products  6.81 us (1%)
    all_gather x1, waiting for transfers between devices, body(): lax.all_gather(picked, 'row', axis=1, tiled=True)  219 us
    reduce_scatter x1, waiting for transfers between devices, body(): lax.psum_scatter(partial_value, 'col', scatter_dimension=1, tiled=True)  152 us
    all_gather x1, waiting for transfers between devices, body(): gathered = lax.all_gather(panel, 'col', axis=1, tiled=True)  92.1 us
  transfers between devices with their start and end apart: 3, of which 3 were waited for; matrix products, arithmetic and copies ran while one was open for 0% of the time, Pallas kernels for 0%

commit v1 on v0

--- a/solution.py
+++ b/solution.py
@@ -27,7 +27,9 @@
     )
     partial_value = jnp.dot(
         anc_inv,
-        lax.all_gather(picked, "row", axis=1, tiled=True),
+        jnp.concatenate(
+            lax.all_to_all(jnp.stack([picked] * lax.axis_size("row")), "row", 0, 0), axis=1
+        ),
         preferred_element_type=jnp.float32,
     )
     summed = lax.psum_scatter(partial_value, "col", scatter_dimension=1, tiled=True)

time: 496 us -> 464 us (0.935)
  waiting for transfers between devices: 463 us -> 242 us
  blocking collectives: 0 us -> 191 us
    all_gather x1 -> x0, waiting for transfers between devices: 219 us -> none  [body(): lax.all_gather(picked, 'row', axis=1, tiled=True)]
    all_to_all x0 -> x1, blocking collectives: none -> 191 us  [body(): lax.all_to_all(jnp.stack([picked] * lax.axis_size('row')), 'row', 0, 0)]
  transfers between devices with their start and end apart: 3 -> 2, of which waited for: 3 -> 2; matrix products, arithmetic and copies ran while one was open for 0% -> 0% of each run, Pallas kernels for 0% -> 0%
where the time goes in v1:
time: 464 us
  waiting for transfers between devices  242 us (52%)
  blocking collectives  191 us (41%)
  between operations  13.5 us (3%)
  local copies, waits for them, and re-layouts  10.8 us (2%)
  matrix products  4.65 us (1%)
    all_to_all x1, blocking collectives, body(): lax.all_to_all(jnp.stack([picked] * lax.axis_size('row')), 'row', 0, 0)  191 us
    reduce_scatter x1, waiting for transfers between devices, body(): lax.psum_scatter(partial_value, 'col', scatter_dimension=1, tiled=True)  149 us
    all_gather x1, waiting for transfers between devices, body(): gathered = lax.all_gather(panel, 'col', axis=1, tiled=True)  92.1 us
  transfers between devices with their start and end apart: 2, of which 2 were waited for; matrix products, arithmetic and copies ran while one was open for 0% of the time, Pallas kernels for 0%

profile of v1, /device:TPU:2, one launch (start us, length us, event | category | flops | bytes accessed | tf_op | source)
XLA Modules:
  0.0 463.7 jit_solution(12561558436711246192)
XLA Ops:
  6.5 0.0 copy-start
  6.5 0.0 all-gather.2.cloned.1.call-start
  6.5 0.7 all-gather.2.cloned.1.call-update
  7.3 0.0 reduce-scatter.2.cloned.1.call-start
  7.3 0.7 subtract_bitcast_fusion
  8.0 92.1 %all-gather.2.cloned.1.call-done = bf16[1,12288,64]{1,2,0:T(8,128)(2,1)} async-done(((bf16[1,768,64]{1,2,0:T(8,128)(2,1)}), bf16[1,12288,64]{1,2,0:T(8,128)(2,1)}) %all-gather.2.cloned.1.call-update) | async-done | bytes 1572880 | tf_op jit(solution)/shard_map/all_gather | solution.py:16
  100.1 4.1 copy.8
  104.2 4.3 reshape_squeeze.3
  108.5 0.3 convolution_convert_fusion
  108.8 0.3 stack_reshape.2
  109.0 0.1 copy.9
  109.2 0.5 stack.6
  109.7 191.0 %all_to_all.5 = bf16[32,1024,64]{1,2,0:T(8,128)(2,1)S(1)} all-to-all(bf16[32,1024,64]{1,2,0:T(8,128)(2,1)S(1)} %stack.6), channel_id=1, replica_groups=mesh['row'=32,'col'=16] {'row'}, dimensions={0} | all-to-all | bytes 8388608 | tf_op jit(solution)/shard_map/all_to_all | solution.py:31
  300.7 0.0 copy-done
  300.7 4.3 convolution_bitcast_fusion
  305.0 0.0 copy-start.1
  305.0 0.0 reduce-scatter.2.cloned.1.call-update
  305.1 0.6 copy-done.1
  305.7 0.2 compare_reduce_fusion
  305.9 0.1 broadcast_bitcast_fusion
  305.9 149.1 %reduce-scatter.2.cloned.1.call-done = f32[512,128]{0,1:T(8,128)} async-done(((f32[512,2048]{0,1:T(8,128)}), f32[512,128]{0,1:T(8,128)}) %reduce-scatter.2.cloned.1.call-update) | async-done | bytes 262160 | tf_op jit(solution)/shard_map/reduce_scatter | solution.py:35
  455.1 1.0 select_bitcast_fusion
  456.0 0.8 copy.10
  (1 shorter events, 0.0 us)
Async XLA Ops:
  6.5 294.1 %copy-start = (bf16[512,1024]{1,0:T(8,128)(2,1)S(1)}, bf16[512,1024]{1,0:T(8,128)(2,1)}, u32[]{:S(2)}) copy-start(bf16[512,1024]{1,0:T(8,128)(2,1)} %param.3) | copy-start | bytes 3145732
  6.5 93.5 %all-gather.2.cloned.1.call-start = ((), (), s32[]{:S(2)}) async-start(), calls=%async_computation.2 | async-start | bytes 1671168 | tf_op jit(solution)/shard_map/all_gather | solution.py:16
  7.3 447.8 %reduce-scatter.2.cloned.1.call-start = ((), (), s32[]{:S(2)}) async-start(), calls=%async_computation.3 | async-start | bytes 4456448 | tf_op jit(solution)/shard_map/reduce_scatter | solution.py:35
  305.0 0.7 copy-start.1
Sparse Core Ops, SparseCore 0:
  10.6 89.3 all-gather.1
  305.2 149.8 reduce-scatter.1
